TPU v7x, 512 devices: a whole 4x8x8 slice. The times are simulated.
512 devices in a mesh: rows: 32 (over y, x), vocab: 16 (over z, core).
Axes of the slice: x: 4, y: 8, z: 8, core: 2. Of those that a mesh axis runs over, the one named last changes fastest.
Arguments:
- hidden: bfloat16 [12288, 8192], P('rows', 'vocab'), may hold values from -128 to 128
- head: bfloat16 [8192, 8192], P('rows', 'vocab'), may hold values from -4 to 4
- targets: int32 [12288], P('rows'), may hold values from 0 to 128255
- live: int32 [12288], P('rows'), may hold values from 0 to 1, as said below
- prior_lse: float32 [12288], P('rows'), may hold values from 10 to 18
- prior_mean: float32 [12288], P('rows'), may hold values from 2 to 8
- prior_target: float32 [12288], P('rows'), may hold values from -12 to 12
- seq_lengths: int32 [32], replicated, may hold values from 1 to 768, 12288 in all
Outputs:
- logprob: float32 [12288], P(('rows', 'vocab'))
- entropy: float32 [12288], P(('rows', 'vocab'))
- seq_score: float32 [32], replicated
Inputs may be any that keep to these rules, and one draw needn't show every extreme that they name: Within the 384 rows of each index of rows, the live rows come first; every such index has at least 48 live rows and some index has all 384.
All inputs are finite; a program needn't handle non-finite values.
Results may differ from a plain program's by a relative error of at most 0.0003.
Values may be sent and summed in bfloat16 or wider, within the bound.
No kernel may reach another device: no remote copies, remote signals or barrier semaphores. Data moves between devices by JAX's collectives and lax.ppermute only.
A program may use at most 64 MiB of HBM per device.

v0:
```python
import jax
import jax.numpy as jnp
from jax import lax
from jax.sharding import PartitionSpec as P

VOCAB = 128256
SEQS = 32
GSIZE = 8


def finish_rows(block_peak, block_mass, block_moment, block_target, live, prior_lse, prior_mean):
    highest = jnp.maximum(block_peak, prior_lse)
    earlier = jnp.exp(prior_lse - highest)
    scaled = jnp.exp(block_peak - highest)
    total_mass = earlier + block_mass * scaled
    norm_log = highest + jnp.log(total_mass)
    average = (earlier * prior_mean + scaled * block_moment) / total_mass
    keeping = live.astype(jnp.float32)
    return (keeping * (block_target - norm_log), keeping * (norm_log - average))


def local(hidden, head, targets, live, prior_lse, prior_mean, prior_target, seq_lengths):
    rows_here = hidden.shape[0]
    cols_here = head.shape[1]
    spread = lax.axis_size("vocab")
    which = lax.axis_index("vocab")
    block_first = VOCAB - cols_here * spread
    first_col = block_first + which * cols_here
    gathered = lax.all_gather(hidden, "vocab", axis=1, tiled=True)
    logits = jnp.dot(
        gathered,
        lax.all_gather(head, "rows", axis=0, tiled=True),
        preferred_element_type=jnp.float32,
    )
    row_peak = jnp.max(logits, axis=1)
    weights = jnp.exp(logits - row_peak[:, None])
    row_mass = jnp.sum(weights, axis=1)
    moment = jnp.sum(weights * logits, axis=1)
    column = targets - first_col
    columns = lax.broadcasted_iota(jnp.int32, logits.shape, 1)
    picked = jnp.sum(jnp.where(columns == column[:, None], logits, jnp.zeros_like(logits)), axis=1)
    stats = jnp.stack([row_peak, row_mass, moment, picked])
    every = lax.all_gather(stats, "vocab", axis=0, tiled=False)
    peaks = every[:, 0]
    highest = jnp.max(peaks, axis=0)
    factor = jnp.exp(peaks - highest[None, :])
    mass_all = jnp.sum(every[:, 1] * factor, axis=0)
    moment_all = jnp.sum(every[:, 2] * factor, axis=0)
    picked_all = jnp.sum(every[:, 3], axis=0)
    block_target = jnp.where(targets >= block_first, picked_all, prior_target)
    logprob, entropy = finish_rows(
        highest, mass_all, moment_all, block_target, live, prior_lse, prior_mean
    )
    share = rows_here // spread
    begin = which * share
    logprob_share = lax.dynamic_slice_in_dim(logprob, begin, share, 0)
    entropy_share = lax.dynamic_slice_in_dim(entropy, begin, share, 0)
    global_rows = lax.axis_index("rows") * rows_here + jnp.arange(rows_here, dtype=jnp.int32)
    endings = jnp.cumsum(seq_lengths)
    member = jnp.sum((global_rows[:, None] >= endings[None, :]).astype(jnp.int32), axis=1)
    onehot = (member[:, None] == jnp.arange(SEQS, dtype=jnp.int32)[None, :]).astype(jnp.float32)
    partial_sums = jnp.sum(onehot * logprob[:, None], axis=0)
    sums = jnp.sum(lax.all_gather(partial_sums, "rows", axis=0, tiled=False), axis=0)
    seq_mean = sums / seq_lengths.astype(jnp.float32)
    grouped = seq_mean.reshape(SEQS // GSIZE, GSIZE)
    seq_score = (grouped - jnp.mean(grouped, axis=1, keepdims=True)).reshape(SEQS)
    return (logprob_share, entropy_share, seq_score)


def solution(mesh):
    return jax.shard_map(
        local,
        mesh=mesh,
        in_specs=(
            P("rows", "vocab"),
            P("rows", "vocab"),
            P("rows"),
            P("rows"),
            P("rows"),
            P("rows"),
            P("rows"),
            P(),
        ),
        out_specs=(P(("rows", "vocab")), P(("rows", "vocab")), P()),
        check_vma=False,
    )
```

profile of v0, /device:TPU:2, one launch (start us, length us, event | category | flops | bytes accessed | tf_op | source)
XLA Modules:
  0.0 275.6 jit_solution(6936003982868174059)
XLA Ops:
  7.2 0.0 all-gather.6.cloned.1.call-start
  7.2 0.7 all-gather.6.cloned.1.call-update
  7.9 0.0 all-gather.8.cloned.1.call-start
  7.9 0.7 all-gather.8.cloned.1.call-update
  8.7 0.7 copy.22
  9.4 0.1 reduce-window.8
  9.5 0.1 reduce.2
  9.6 1.3 dynamic-slice
  11.5 0.1 convert_reduce_fusion
  11.6 0.7 broadcast_subtract_fusion
  12.3 0.0 copy-start.4
  12.3 0.0 copy-start.5
  12.3 52.0 %all-gather.6.cloned.1.call-done = bf16[384,8192]{1,0:T(8,128)(2,1)} async-done(((bf16[384,512]{1,0:T(8,128)(2,1)}), bf16[384,8192]{1,0:T(8,128)(2,1)}) %all-gather.6.cloned.1.call-update) | async-done | bytes 6291472 | tf_op jit(solution)/shard_map/all_gather | solution.py:29
  64.3 103.5 %all-gather.8.cloned.1.call-done = bf16[8192,512]{1,0:T(8,128)(2,1)} async-done(((bf16[256,512]{1,0:T(8,128)(2,1)}), bf16[8192,512]{1,0:T(8,128)(2,1)}) %all-gather.8.cloned.1.call-update) | async-done | bytes 8388624 | tf_op jit(solution)/shard_map/all_gather | solution.py:32
  167.7 8.0 %fusion.7 = (f32[384]{0:T(512)S(1)}, f32[384,512]{1,0:T(8,128)S(1)}) fusion(bf16[384,8192]{1,0:T(8,128)(2,1)} %all-gather.6.cloned.1.call-done, bf16[8192,512]{1,0:T(8,128)(2,1)} %all-gather.8.cloned.1.call-done), kind=kOutput, calls=%fused_computation.30 | convolution fusion | flops 3221421568 | bytes 15468032 | tf_op jit(solution)/shard_map/dot_general | solution.py:30
  175.8 0.5 fusion
  176.3 18.3 %all-gather.2 = f32[16,4,384]{2,1,0:T(4,128)S(1)} all-gather(f32[1,4,384]{2,1,0:T(4,128)S(1)} %maximum_bitcast_fusion), channel_id=2, replica_groups=mesh['rows'=32,'vocab'=16] {'vocab'}, dimensions={0}, use_global_device_ids=true | all-gather | bytes 104448 | tf_op jit(solution)/shard_map/all_gather | solution.py:43
  194.6 0.1 fusion.6
  194.8 0.0 copy-done
  194.8 0.0 copy-done.1
  194.8 0.6 dynamic_slice.6
  195.4 0.6 dynamic_slice.7
  196.0 0.1 select_reduce_fusion.1
  196.1 0.2 dynamic-update-slice
  196.4 71.4 %all-reduce = f32[1024]{0:T(1024)S(1)} all-reduce(f32[1024]{0:T(1024)S(1)} %dynamic-update-slice), channel_id=3, replica_groups=mesh['rows'=32,'vocab'=16] {'rows'}, use_global_device_ids=true, to_apply=%add | all-reduce | flops 1024 | bytes 8192
  267.8 0.1 reshape.52
  267.9 0.0 copy-done.5
  267.9 0.1 reshape.50
  268.0 0.1 reduce_sum.99
  268.1 0.1 sub.55
  268.2 0.1 sub.56
  268.2 0.5 sub.57
  (19 shorter events, 0.1 us)
Async XLA Ops:
  7.2 57.1 %all-gather.6.cloned.1.call-start = ((), (), s32[]{:S(2)}) async-start(), calls=%async_computation | async-start | bytes 6684672 | tf_op jit(solution)/shard_map/all_gather | solution.py:29
  7.9 159.8 %all-gather.8.cloned.1.call-start = ((), (), s32[]{:S(2)}) async-start(), calls=%async_computation.1 | async-start | bytes 8650752 | tf_op jit(solution)/shard_map/all_gather | solution.py:32
  12.3 182.5 %copy-start = (s32[384]{0:T(512)S(1)}, s32[384]{0:T(512)}, u32[]{:S(2)}) copy-start(s32[384]{0:T(512)} %param.10) | copy-start | bytes 4612
  12.3 182.5 %copy-start.1 = (f32[384]{0:T(512)S(1)}, f32[384]{0:T(512)}, u32[]{:S(2)}) copy-start(f32[384]{0:T(512)} %param.13) | copy-start | bytes 4612
  12.3 182.5 %copy-start.2 = (s32[384]{0:T(512)S(1)}, s32[384]{0:T(512)}, u32[]{:S(2)}) copy-start(s32[384]{0:T(512)} %param.11) | copy-start | bytes 4612
  12.3 182.5 %copy-start.3 = (f32[384]{0:T(512)S(1)}, f32[384]{0:T(512)}, u32[]{:S(2)}) copy-start(f32[384]{0:T(512)} %param.12) | copy-start | bytes 4612
  12.3 182.5 %copy-start.4 = (f32[384]{0:T(512)S(1)}, f32[384]{0:T(512)}, u32[]{:S(2)}) copy-start(f32[384]{0:T(512)} %param.14) | copy-start | bytes 4612
  12.3 255.5 %copy-start.5 = (s32[32]{0:T(128)S(1)}, s32[32]{0:T(128)}, u32[]{:S(2)}) copy-start(s32[32]{0:T(128)} %param.15) | copy-start | bytes 388
Sparse Core Ops, SparseCore 0:
  10.1 54.0 all-gather.5
  67.4 100.2 all-gather.7
where the time goes:
time: 276 us
  waiting for transfers between devices  157 us (57%)
  blocking collectives  89.7 us (32%)
  between operations  14.8 us (5%)
  matrix products  8 us (3%)
  local copies, waits for them, and re-layouts  3.78 us (1%)
    all_gather x1, waiting for transfers between devices, local(): lax.all_gather(head, 'rows', axis=0, tiled=True)  103 us
    unnamed x1, blocking collectives  71.4 us
    all_gather x1, waiting for transfers between devices, local(): gathered = lax.all_gather(hidden, 'vocab', axis=1, tiled=True)  52 us
    all_gather x1, blocking collectives, local(): every = lax.all_gather(stats, 'vocab', axis=0, tiled=False)  18.3 us
    dot_general x1, matrix products, local(): jnp.dot(gathered, lax.all_gather(head, 'rows', axis=0, tiled=True), prefe...  8 us
  transfers between devices with their start and end apart: 2, of which 2 were waited for; matrix products, arithmetic and copies ran while one was open for 1% of the time, Pallas kernels for 0%

commit v1 on v0

--- a/solution.py
+++ b/solution.py
@@ -6,6 +6,28 @@
 VOCAB = 128256
 SEQS = 32
 GSIZE = 8
+
+
+def laid_out(blocks, dim):
+    blocks = jnp.moveaxis(blocks, 0, dim)
+    shape = blocks.shape
+    return blocks.reshape(*shape[:dim], shape[dim] * shape[dim + 1], *shape[dim + 2 :])
+
+
+def ring_gather(shard, axis, dim):
+    devices = lax.axis_size(axis)
+    pairs = [(i, (i + 1) % devices) for i in range(devices)]
+    back = [(b, a) for a, b in pairs]
+    lower, upper = ([], [])
+    for step in range(devices - 1):
+        if step % 2 == 0:
+            lower.append(lax.ppermute(lower[-1] if lower else shard, axis, pairs))
+        else:
+            upper.append(lax.ppermute(upper[-1] if upper else shard, axis, back))
+    blocks = jnp.stack([*lower[::-1], shard, *upper])
+    shift = lax.axis_index(axis) - len(lower)
+    blocks = blocks[(jnp.arange(devices) - shift) % devices]
+    return laid_out(blocks, dim)
 
 
 def finish_rows(block_peak, block_mass, block_moment, block_target, live, prior_lse, prior_mean):
@@ -26,7 +48,7 @@
     which = lax.axis_index("vocab")
     block_first = VOCAB - cols_here * spread
     first_col = block_first + which * cols_here
-    gathered = lax.all_gather(hidden, "vocab", axis=1, tiled=True)
+    gathered = ring_gather(hidden, "vocab", 1)
     logits = jnp.dot(
         gathered,
         lax.all_gather(head, "rows", axis=0, tiled=True),

time: 276 us -> 227 us (0.82)
  waiting for transfers between devices: 157 us -> 48.5 us
  local copies, waits for them, and re-layouts: 3.78 us -> 37.8 us
  starting transfers between devices: 0.08 us -> 21.4 us
  other arithmetic: 2.39 us -> 5.54 us
    all_gather x1, waiting for transfers between devices: 103 us -> 2.08 us  [local(): lax.all_gather(head, 'rows', axis=0, tiled=True)]
    all_gather x1 -> x0, waiting for transfers between devices: 52 us -> none  [local(): gathered = lax.all_gather(hidden, 'vocab', axis=1, tiled=True)]
    ppermute x0 -> x15, waiting for transfers between devices: none -> 45.7 us  [the longest x8 45 us: ring_gather(): lower.append(lax.ppermute(lower[-1] if lower else shard, axis, pairs))]
    ppermute x0 -> x15, starting transfers between devices: none -> 21.4 us  [the longest x7 21.3 us: ring_gather(): upper.append(lax.ppermute(upper[-1] if upper else shard, axis, back))]
    unnamed x15 -> x34, local copies, waits for them, and re-layouts: 1.55 us -> 19.7 us
    transpose x0 -> x1, local copies, waits for them, and re-layouts: none -> 8.61 us  [laid_out(): blocks = jnp.moveaxis(blocks, 0, dim)]
    gather x0 -> x1, local copies, waits for them, and re-layouts: none -> 6.46 us  [ring_gather(): blocks = blocks[(jnp.arange(devices) - shift) % devices]]
  transfers between devices with their start and end apart: 2 -> 16, of which waited for: 2 -> 10; matrix products, arithmetic and copies ran while one was open for 1% -> 18% of each run, Pallas kernels for 0% -> 0%
where the time goes in v1:
time: 227 us; the launch traced here: 226 us
  blocking collectives  89.7 us (40%)
  waiting for transfers between devices  48.5 us (21%)
  local copies, waits for them, and re-layouts  37.8 us (17%)
  starting transfers between devices  21.4 us (9%)
  between operations  14.9 us (7%)
  matrix products  8.12 us (4%)
  other arithmetic  5.54 us (2%)
    unnamed x1, blocking collectives  71.4 us
    ppermute x8, waiting for transfers between devices, ring_gather(): lower.append(lax.ppermute(lower[-1] if lower else shard, axis, pairs))  45 us
    ppermute x7, starting transfers between devices, ring_gather(): upper.append(lax.ppermute(upper[-1] if upper else shard, axis, back))  21.3 us
    unnamed x34, local copies, waits for them, and re-layouts  19.7 us
    all_gather x1, blocking collectives, local(): every = lax.all_gather(stats, 'vocab', axis=0, tiled=False)  18.3 us
    transpose x1, local copies, waits for them, and re-layouts, laid_out(): blocks = jnp.moveaxis(blocks, 0, dim)  8.61 us
    dot_general x1, matrix products, local(): jnp.dot(gathered, lax.all_gather(head, 'rows', axis=0, tiled=True), prefe...  8.12 us
    gather x1, local copies, waits for them, and re-layouts, ring_gather(): blocks = blocks[(jnp.arange(devices) - shift) % devices]  6.46 us
  transfers between devices with their start and end apart: 16, of which 10 were waited for; matrix products, arithmetic and copies ran while one was open for 18% of the time, Pallas kernels for 0%

profile of v1, /device:TPU:2, one launch (start us, length us, event | category | flops | bytes accessed | tf_op | source)
XLA Modules:
  0.0 225.9 jit_solution(264909723769320608)
XLA Ops:
  7.9 14.1 %collective-permute-done = bf16[384,512]{1,0:T(8,128)(2,1)S(1)} collective-permute-done((bf16[384,512]{1,0:T(8,128)(2,1)}, bf16[384,512]{1,0:T(8,128)(2,1)S(1)}, u32[]{:S(2)}, u32[]{:S(2)}) %collective-permute-start) | collective-permute-done | bytes 393248 | tf_op jit(solution)/shard_map/ppermute | solution.py:24
  22.1 3.0 %collective-permute-start.8 = (bf16[384,512]{1,0:T(8,128)(2,1)}, bf16[384,512]{1,0:T(8,128)(2,1)S(1)}, u32[]{:S(2)}, u32[]{:S(2)}) collective-permute-start(bf16[384,512]{1,0:T(8,128)(2,1)} %param.8), channel_id=1, source_target_pairs={{1,0},{2,1},{3,2},{4,3},{5,4},{6,5},{7,6},{8,7},{9,8},{10,9},{11,1... | collective-permute-start | bytes 1179656 | tf_op jit(solution)/shard_map/ppermute | solution.py:26
  25.0 5.5 %collective-permute-done.1 = bf16[384,512]{1,0:T(8,128)(2,1)S(1)} collective-permute-done((bf16[384,512]{1,0:T(8,128)(2,1)S(1)}, bf16[384,512]{1,0:T(8,128)(2,1)S(1)}, u32[]{:S(2)}, u32[]{:S(2)}) %collective-permute-start.1) | collective-permute-done | bytes 393248 | tf_op jit(solution)/shard_map/ppermute | solution.py:24
  30.6 3.0 %collective-permute-start.9 = (bf16[384,512]{1,0:T(8,128)(2,1)S(1)}, bf16[384,512]{1,0:T(8,128)(2,1)S(1)}, u32[]{:S(2)}, u32[]{:S(2)}) collective-permute-start(bf16[384,512]{1,0:T(8,128)(2,1)S(1)} %collective-permute-done.8), channel_id=1, source_target_pairs={{1,0},{2,1},{3,2},{4,3},{5,4},{6,5},{7,6},{8,7},{9,8},{10,9},{11,1... | collective-permute-start | bytes 1179656 | tf_op jit(solution)/shard_map/ppermute | solution.py:26
  33.7 5.2 %collective-permute-done.2 = bf16[384,512]{1,0:T(8,128)(2,1)S(1)} collective-permute-done((bf16[384,512]{1,0:T(8,128)(2,1)S(1)}, bf16[384,512]{1,0:T(8,128)(2,1)S(1)}, u32[]{:S(2)}, u32[]{:S(2)}) %collective-permute-start.2) | collective-permute-done | bytes 393248 | tf_op jit(solution)/shard_map/ppermute | solution.py:24
  38.9 3.1 %collective-permute-start.10 = (bf16[384,512]{1,0:T(8,128)(2,1)S(1)}, bf16[384,512]{1,0:T(8,128)(2,1)S(1)}, u32[]{:S(2)}, u32[]{:S(2)}) collective-permute-start(bf16[384,512]{1,0:T(8,128)(2,1)S(1)} %collective-permute-done.9), channel_id=1, source_target_pairs={{1,0},{2,1},{3,2},{4,3},{5,4},{6,5},{7,6},{8,7},{9,8},{10,9},{11,1... | collective-permute-start | bytes 1179656 | tf_op jit(solution)/shard_map/ppermute | solution.py:26
  42.1 5.2 %collective-permute-done.3 = bf16[384,512]{1,0:T(8,128)(2,1)S(1)} collective-permute-done((bf16[384,512]{1,0:T(8,128)(2,1)S(1)}, bf16[384,512]{1,0:T(8,128)(2,1)S(1)}, u32[]{:S(2)}, u32[]{:S(2)}) %collective-permute-start.3) | collective-permute-done | bytes 393248 | tf_op jit(solution)/shard_map/ppermute | solution.py:24
  47.4 3.5 %collective-permute-start.11 = (bf16[384,512]{1,0:T(8,128)(2,1)S(1)}, bf16[384,512]{1,0:T(8,128)(2,1)S(1)}, u32[]{:S(2)}, u32[]{:S(2)}) collective-permute-start(bf16[384,512]{1,0:T(8,128)(2,1)S(1)} %collective-permute-done.10), channel_id=1, source_target_pairs={{1,0},{2,1},{3,2},{4,3},{5,4},{6,5},{7,6},{8,7},{9,8},{10,9},{11,1... | collective-permute-start | bytes 1179656 | tf_op jit(solution)/shard_map/ppermute | solution.py:26
  50.9 4.8 %collective-permute-done.4 = bf16[384,512]{1,0:T(8,128)(2,1)S(1)} collective-permute-done((bf16[384,512]{1,0:T(8,128)(2,1)S(1)}, bf16[384,512]{1,0:T(8,128)(2,1)S(1)}, u32[]{:S(2)}, u32[]{:S(2)}) %collective-permute-start.4) | collective-permute-done | bytes 393248 | tf_op jit(solution)/shard_map/ppermute | solution.py:24
  56.5 2.8 %collective-permute-start.12 = (bf16[384,512]{1,0:T(8,128)(2,1)S(1)}, bf16[384,512]{1,0:T(8,128)(2,1)}, u32[]{:S(2)}, u32[]{:S(2)}) collective-permute-start(bf16[384,512]{1,0:T(8,128)(2,1)S(1)} %collective-permute-done.11), channel_id=1, source_target_pairs={{1,0},{2,1},{3,2},{4,3},{5,4},{6,5},{7,6},{8,7},{9,8},{10,9},{11,1... | collective-permute-start | bytes 1179656 | tf_op jit(solution)/shard_map/ppermute | solution.py:26
  59.3 4.9 %collective-permute-done.5 = bf16[384,512]{1,0:T(8,128)(2,1)} collective-permute-done((bf16[384,512]{1,0:T(8,128)(2,1)S(1)}, bf16[384,512]{1,0:T(8,128)(2,1)}, u32[]{:S(2)}, u32[]{:S(2)}) %collective-permute-start.5) | collective-permute-done | bytes 393248 | tf_op jit(solution)/shard_map/ppermute | solution.py:24
  64.9 3.0 %collective-permute-start.13 = (bf16[384,512]{1,0:T(8,128)(2,1)}, bf16[384,512]{1,0:T(8,128)(2,1)}, u32[]{:S(2)}, u32[]{:S(2)}) collective-permute-start(bf16[384,512]{1,0:T(8,128)(2,1)} %collective-permute-done.12), channel_id=1, source_target_pairs={{1,0},{2,1},{3,2},{4,3},{5,4},{6,5},{7,6},{8,7},{9,8},{10,9},{11,1... | collective-permute-start | bytes 1179656 | tf_op jit(solution)/shard_map/ppermute | solution.py:26
  67.8 5.2 %collective-permute-done.6 = bf16[384,512]{1,0:T(8,128)(2,1)} collective-permute-done((bf16[384,512]{1,0:T(8,128)(2,1)}, bf16[384,512]{1,0:T(8,128)(2,1)}, u32[]{:S(2)}, u32[]{:S(2)}) %collective-permute-start.6) | collective-permute-done | bytes 393248 | tf_op jit(solution)/shard_map/ppermute | solution.py:24
  74.9 0.8 reduce.2
  75.8 1.3 dynamic-slice
  79.1 3.0 %collective-permute-start.14 = (bf16[384,512]{1,0:T(8,128)(2,1)}, bf16[384,512]{1,0:T(8,128)(2,1)S(1)}, u32[]{:S(2)}, u32[]{:S(2)}) collective-permute-start(bf16[384,512]{1,0:T(8,128)(2,1)} %collective-permute-done.13), channel_id=1, source_target_pairs={{1,0},{2,1},{3,2},{4,3},{5,4},{6,5},{7,6},{8,7},{9,8},{10,9},{11,1... | collective-permute-start | bytes 1179656 | tf_op jit(solution)/shard_map/ppermute | solution.py:26
  82.1 1.8 bitcast_dynamic-update-slice_fusion.15
  83.9 1.8 bitcast_dynamic-update-slice_fusion.14
  85.7 1.8 bitcast_dynamic-update-slice_fusion.13
  87.5 1.8 bitcast_dynamic-update-slice_fusion.12
  90.1 0.8 bitcast_dynamic-update-slice_fusion.10
  90.9 0.8 bitcast_dynamic-update-slice_fusion.9
  91.7 0.8 bitcast_dynamic-update-slice_fusion.8
  95.6 0.8 bitcast_dynamic-update-slice_fusion.3
  96.4 1.8 bitcast_dynamic-update-slice_fusion.2
  98.2 1.8 bitcast_dynamic-update-slice_fusion.1
  100.8 6.5 %gather_fusion = bf16[16,384,512]{2,1,0:T(8,128)(2,1)} fusion(bf16[16,384,512]{2,1,0:T(8,128)(2,1)} %bitcast_dynamic-update-slice_fusion, s32[1024]{0:T(1024)} %pad_clamp_fusion), kind=kCustom, calls=%fused_computation | custom fusion | bytes 12582976 | tf_op jit(solution)/shard_map/gather | solution.py:29
  107.2 8.6 %copy.25 = bf16[384,16,512]{0,2,1:T(8,128)(2,1)} copy(bf16[384,16,512]{2,0,1:T(8,128)(2,1)} %bitcast.63) | data formatting | bytes 12582912 | tf_op jit(solution)/shard_map/transpose | solution.py:12
  115.8 2.1 all-gather.5.cloned.1.call-done
  117.9 8.1 %fusion.9 = (f32[384]{0:T(512)S(1)}, f32[384,512]{1,0:T(8,128)S(1)}) fusion(bf16[384,8192]{0,1:T(8,128)(2,1)} %bitcast.62, bf16[8192,512]{1,0:T(8,128)(2,1)} %all-gather.5.cloned.1.call-done), kind=kOutput, calls=%fused_computation.54 | convolution fusion | flops 3221421568 | bytes 15468032 | tf_op jit(solution)/shard_map/dot_general | solution.py:52
  126.6 18.3 %all-gather.2 = f32[16,4,384]{2,1,0:T(4,128)S(1)} all-gather(f32[1,4,384]{2,1,0:T(4,128)S(1)} %maximum_bitcast_fusion), channel_id=2, replica_groups=mesh['rows'=32,'vocab'=16] {'vocab'}, dimensions={0}, use_global_device_ids=true | all-gather | bytes 104448 | tf_op jit(solution)/shard_map/all_gather | solution.py:65
  145.5 71.4 %all-reduce = f32[1024]{0:T(1024)S(1)} all-reduce(f32[1024]{0:T(1024)S(1)} %dynamic-update-slice), channel_id=3, replica_groups=mesh['rows'=32,'vocab'=16] {'rows'}, use_global_device_ids=true, to_apply=%add | all-reduce | flops 1024 | bytes 8192
  (70 shorter events, 13.7 us)
Async XLA Ops:
  7.2 85.3 %copy-start = (bf16[384,512]{1,0:T(8,128)(2,1)S(1)}, bf16[384,512]{1,0:T(8,128)(2,1)}, u32[]{:S(2)}) copy-start(bf16[384,512]{1,0:T(8,128)(2,1)} %param.8) | copy-start | bytes 1179652
  7.2 110.7 %all-gather.5.cloned.1.call-start = ((), (), s32[]{:S(2)}) async-start(), calls=%async_computation | async-start | bytes 8650752 | tf_op jit(solution)/shard_map/all_gather | solution.py:54
  7.9 14.2 %collective-permute-start = (bf16[384,512]{1,0:T(8,128)(2,1)}, bf16[384,512]{1,0:T(8,128)(2,1)S(1)}, u32[]{:S(2)}, u32[]{:S(2)}) collective-permute-start(bf16[384,512]{1,0:T(8,128)(2,1)} %param.8), channel_id=1, source_target_pairs={{0,1},{1,2},{2,3},{3,4},{4,5},{5,6},{6,7},{7,8},{8,9},{9,10},{10,1... | collective-permute-start | bytes 1179656 | tf_op jit(solution)/shard_map/ppermute | solution.py:24
  22.1 8.4 %collective-permute-start.1 = (bf16[384,512]{1,0:T(8,128)(2,1)S(1)}, bf16[384,512]{1,0:T(8,128)(2,1)S(1)}, u32[]{:S(2)}, u32[]{:S(2)}) collective-permute-start(bf16[384,512]{1,0:T(8,128)(2,1)S(1)} %collective-permute-done), channel_id=1, source_target_pairs={{0,1},{1,2},{2,3},{3,4},{4,5},{5,6},{6,7},{7,8},{8,9},{9,10},{10,1... | collective-permute-start | bytes 1179656 | tf_op jit(solution)/shard_map/ppermute | solution.py:24
  22.1 8.6 %collective-permute-start.8 = (bf16[384,512]{1,0:T(8,128)(2,1)}, bf16[384,512]{1,0:T(8,128)(2,1)S(1)}, u32[]{:S(2)}, u32[]{:S(2)}) collective-permute-start(bf16[384,512]{1,0:T(8,128)(2,1)} %param.8), channel_id=1, source_target_pairs={{1,0},{2,1},{3,2},{4,3},{5,4},{6,5},{7,6},{8,7},{9,8},{10,9},{11,1... | collective-permute-start | bytes 1179656 | tf_op jit(solution)/shard_map/ppermute | solution.py:26
  30.5 8.4 %collective-permute-start.2 = (bf16[384,512]{1,0:T(8,128)(2,1)S(1)}, bf16[384,512]{1,0:T(8,128)(2,1)S(1)}, u32[]{:S(2)}, u32[]{:S(2)}) collective-permute-start(bf16[384,512]{1,0:T(8,128)(2,1)S(1)} %collective-permute-done.1), channel_id=1, source_target_pairs={{0,1},{1,2},{2,3},{3,4},{4,5},{5,6},{6,7},{7,8},{8,9},{9,10},{10,1... | collective-permute-start | bytes 1179656 | tf_op jit(solution)/shard_map/ppermute | solution.py:24
  30.6 8.3 %collective-permute-start.9 = (bf16[384,512]{1,0:T(8,128)(2,1)S(1)}, bf16[384,512]{1,0:T(8,128)(2,1)S(1)}, u32[]{:S(2)}, u32[]{:S(2)}) collective-permute-start(bf16[384,512]{1,0:T(8,128)(2,1)S(1)} %collective-permute-done.8), channel_id=1, source_target_pairs={{1,0},{2,1},{3,2},{4,3},{5,4},{6,5},{7,6},{8,7},{9,8},{10,9},{11,1... | collective-permute-start | bytes 1179656 | tf_op jit(solution)/shard_map/ppermute | solution.py:26
  38.9 8.4 %collective-permute-start.3 = (bf16[384,512]{1,0:T(8,128)(2,1)S(1)}, bf16[384,512]{1,0:T(8,128)(2,1)S(1)}, u32[]{:S(2)}, u32[]{:S(2)}) collective-permute-start(bf16[384,512]{1,0:T(8,128)(2,1)S(1)} %collective-permute-done.2), channel_id=1, source_target_pairs={{0,1},{1,2},{2,3},{3,4},{4,5},{5,6},{6,7},{7,8},{8,9},{9,10},{10,1... | collective-permute-start | bytes 1179656 | tf_op jit(solution)/shard_map/ppermute | solution.py:24
  38.9 8.4 %collective-permute-start.10 = (bf16[384,512]{1,0:T(8,128)(2,1)S(1)}, bf16[384,512]{1,0:T(8,128)(2,1)S(1)}, u32[]{:S(2)}, u32[]{:S(2)}) collective-permute-start(bf16[384,512]{1,0:T(8,128)(2,1)S(1)} %collective-permute-done.9), channel_id=1, source_target_pairs={{1,0},{2,1},{3,2},{4,3},{5,4},{6,5},{7,6},{8,7},{9,8},{10,9},{11,1... | collective-permute-start | bytes 1179656 | tf_op jit(solution)/shard_map/ppermute | solution.py:26
  47.3 8.4 %collective-permute-start.4 = (bf16[384,512]{1,0:T(8,128)(2,1)S(1)}, bf16[384,512]{1,0:T(8,128)(2,1)S(1)}, u32[]{:S(2)}, u32[]{:S(2)}) collective-permute-start(bf16[384,512]{1,0:T(8,128)(2,1)S(1)} %collective-permute-done.3), channel_id=1, source_target_pairs={{0,1},{1,2},{2,3},{3,4},{4,5},{5,6},{6,7},{7,8},{8,9},{9,10},{10,1... | collective-permute-start | bytes 1179656 | tf_op jit(solution)/shard_map/ppermute | solution.py:24
  47.4 8.8 %collective-permute-start.11 = (bf16[384,512]{1,0:T(8,128)(2,1)S(1)}, bf16[384,512]{1,0:T(8,128)(2,1)S(1)}, u32[]{:S(2)}, u32[]{:S(2)}) collective-permute-start(bf16[384,512]{1,0:T(8,128)(2,1)S(1)} %collective-permute-done.10), channel_id=1, source_target_pairs={{1,0},{2,1},{3,2},{4,3},{5,4},{6,5},{7,6},{8,7},{9,8},{10,9},{11,1... | collective-permute-start | bytes 1179656 | tf_op jit(solution)/shard_map/ppermute | solution.py:26
  55.7 0.8 copy-start.1
  55.7 8.5 %collective-permute-start.5 = (bf16[384,512]{1,0:T(8,128)(2,1)S(1)}, bf16[384,512]{1,0:T(8,128)(2,1)}, u32[]{:S(2)}, u32[]{:S(2)}) collective-permute-start(bf16[384,512]{1,0:T(8,128)(2,1)S(1)} %collective-permute-done.4), channel_id=1, source_target_pairs={{0,1},{1,2},{2,3},{3,4},{4,5},{5,6},{6,7},{7,8},{8,9},{9,10},{10,1... | collective-permute-start | bytes 1179656 | tf_op jit(solution)/shard_map/ppermute | solution.py:24
  56.5 8.4 %collective-permute-start.12 = (bf16[384,512]{1,0:T(8,128)(2,1)S(1)}, bf16[384,512]{1,0:T(8,128)(2,1)}, u32[]{:S(2)}, u32[]{:S(2)}) collective-permute-start(bf16[384,512]{1,0:T(8,128)(2,1)S(1)} %collective-permute-done.11), channel_id=1, source_target_pairs={{1,0},{2,1},{3,2},{4,3},{5,4},{6,5},{7,6},{8,7},{9,8},{10,9},{11,1... | collective-permute-start | bytes 1179656 | tf_op jit(solution)/shard_map/ppermute | solution.py:26
  64.2 8.7 %collective-permute-start.6 = (bf16[384,512]{1,0:T(8,128)(2,1)}, bf16[384,512]{1,0:T(8,128)(2,1)}, u32[]{:S(2)}, u32[]{:S(2)}) collective-permute-start(bf16[384,512]{1,0:T(8,128)(2,1)} %collective-permute-done.5), channel_id=1, source_target_pairs={{0,1},{1,2},{2,3},{3,4},{4,5},{5,6},{6,7},{7,8},{8,9},{9,10},{10,1... | collective-permute-start | bytes 1179656 | tf_op jit(solution)/shard_map/ppermute | solution.py:24
  64.9 14.3 %collective-permute-start.13 = (bf16[384,512]{1,0:T(8,128)(2,1)}, bf16[384,512]{1,0:T(8,128)(2,1)}, u32[]{:S(2)}, u32[]{:S(2)}) collective-permute-start(bf16[384,512]{1,0:T(8,128)(2,1)} %collective-permute-done.12), channel_id=1, source_target_pairs={{1,0},{2,1},{3,2},{4,3},{5,4},{6,5},{7,6},{8,7},{9,8},{10,9},{11,1... | collective-permute-start | bytes 1179656 | tf_op jit(solution)/shard_map/ppermute | solution.py:26
  73.0 9.1 %collective-permute-start.7 = (bf16[384,512]{1,0:T(8,128)(2,1)}, bf16[384,512]{1,0:T(8,128)(2,1)}, u32[]{:S(2)}, u32[]{:S(2)}) collective-permute-start(bf16[384,512]{1,0:T(8,128)(2,1)} %collective-permute-done.6), channel_id=1, source_target_pairs={{0,1},{1,2},{2,3},{3,4},{4,5},{5,6},{6,7},{7,8},{8,9},{9,10},{10,1... | collective-permute-start | bytes 1179656 | tf_op jit(solution)/shard_map/ppermute | solution.py:24
  79.1 20.8 %collective-permute-start.14 = (bf16[384,512]{1,0:T(8,128)(2,1)}, bf16[384,512]{1,0:T(8,128)(2,1)S(1)}, u32[]{:S(2)}, u32[]{:S(2)}) collective-permute-start(bf16[384,512]{1,0:T(8,128)(2,1)} %collective-permute-done.13), channel_id=1, source_target_pairs={{1,0},{2,1},{3,2},{4,3},{5,4},{6,5},{7,6},{8,7},{9,8},{10,9},{11,1... | collective-permute-start | bytes 1179656 | tf_op jit(solution)/shard_map/ppermute | solution.py:26
  117.9 27.2 %copy-start.2 = (s32[384]{0:T(512)S(1)}, s32[384]{0:T(512)}, u32[]{:S(2)}) copy-start(s32[384]{0:T(512)} %param.10) | copy-start | bytes 4612
  117.9 27.2 %copy-start.3 = (f32[384]{0:T(512)S(1)}, f32[384]{0:T(512)}, u32[]{:S(2)}) copy-start(f32[384]{0:T(512)} %param.13) | copy-start | bytes 4612
  117.9 27.2 %copy-start.4 = (s32[384]{0:T(512)S(1)}, s32[384]{0:T(512)}, u32[]{:S(2)}) copy-start(s32[384]{0:T(512)} %param.11) | copy-start | bytes 4612
  117.9 27.2 %copy-start.5 = (f32[384]{0:T(512)S(1)}, f32[384]{0:T(512)}, u32[]{:S(2)}) copy-start(f32[384]{0:T(512)} %param.12) | copy-start | bytes 4612
  117.9 27.2 %copy-start.6 = (f32[384]{0:T(512)S(1)}, f32[384]{0:T(512)}, u32[]{:S(2)}) copy-start(f32[384]{0:T(512)} %param.14) | copy-start | bytes 4612
  117.9 99.1 %copy-start.7 = (s32[32]{0:T(128)S(1)}, s32[32]{0:T(128)}, u32[]{:S(2)}) copy-start(s32[32]{0:T(128)} %param.15) | copy-start | bytes 388
Sparse Core Ops, SparseCore 0:
  11.2 106.6 all-gather.4
